TPU v7x, 32 devices: a whole 2x2x4 slice. The times are simulated.
32 devices in a mesh: group: 2 (over y), inp: 4 (over z), tm: 2 (over x), pol: 2 (over core).
Axes of the slice: x: 2, y: 2, z: 4, core: 2. Of those that a mesh axis runs over, the one named last changes fastest.
Arguments:
- voltages: bfloat16 [1024, 65536], P(('group', 'inp'), ('tm', 'pol')), parts along dimension 0, may hold values from -6 to 6
Outputs:
- visibilities: float32 [1024, 2, 512, 512], P(('group', 'inp', 'tm'), None, 'pol'), parts along dimension 0
There are 2 independent parts, one for each index of `group`. A program takes and returns all parts, laid end to end along the dimension named above; each array names one. Nothing has to cross between parts.
All inputs are finite; a program needn't handle non-finite values.
Results may differ from a plain program's by a relative error of at most 0.0054.
Values may be sent and summed in bfloat16 or wider, within the bound.
No kernel may reach another device: no remote copies, remote signals or barrier semaphores. Data moves between devices by JAX's collectives and lax.ppermute only.
A program may use at most 256 MiB of HBM per device.

v0:
```python
import math
import jax
import jax.numpy as jnp
from jax import lax
from jax.sharding import PartitionSpec as P

CH = 512
TAPS = 16


def shifted(block, axis, distance):
    devices = range(lax.axis_size(axis))
    route = [(i - distance, i) for i in devices if i - distance in devices]
    return lax.ppermute(block, axis, route)


def prototype(tap_count, frame_len):
    length = tap_count * frame_len
    sample = lax.broadcasted_iota(jnp.int32, (length,), 0).astype(jnp.float32)
    centred = (sample - (length - 1) / 2.0) / frame_len
    window = 0.5 - 0.5 * jnp.cos(2.0 * math.pi * (sample + 0.5) / length)
    angle = math.pi * centred
    filter_taps = jnp.sin(angle) / angle * window
    filter_taps = filter_taps / jnp.sqrt(jnp.sum(filter_taps * filter_taps))
    return filter_taps.reshape(tap_count, frame_len)


def dft_table(frame_len):
    sample_idx = lax.broadcasted_iota(jnp.int32, (frame_len, frame_len // 2), 0)
    channel_idx = lax.broadcasted_iota(jnp.int32, (frame_len, frame_len // 2), 1)
    phase = (sample_idx * channel_idx % frame_len).astype(jnp.float32) * (2.0 * math.pi / frame_len)
    table = jnp.stack([jnp.cos(phase), -jnp.sin(phase)], axis=2)
    return table.reshape(frame_len, frame_len).astype(jnp.bfloat16)


def per_device(voltages):
    inputs_here = voltages.shape[0]
    frame_len = 2 * CH
    frames = voltages.reshape(inputs_here, voltages.shape[1] // frame_len, frame_len)
    spectra_here = frames.shape[1]
    last_frames = frames[:, spectra_here - (TAPS - 1) :, :]
    history = shifted(last_frames, ("tm", "pol"), 1)
    extended = jnp.concatenate([history, frames], axis=1)
    filter_taps = prototype(TAPS, frame_len)
    filtered = jnp.zeros((inputs_here, spectra_here, frame_len), jnp.float32)
    for tap_index in range(TAPS):
        filtered = filtered + filter_taps[tap_index] * extended[
            :, tap_index : tap_index + spectra_here, :
        ].astype(jnp.float32)
    filtered = filtered.astype(jnp.bfloat16)
    spectra = lax.dot_general(
        dft_table(frame_len),
        filtered.reshape(inputs_here * spectra_here, frame_len),
        (((0,), (1,)), ((), ())),
        preferred_element_type=jnp.float32,
    )
    spectra = spectra.astype(jnp.bfloat16).reshape(CH, 2, inputs_here, spectra_here)
    inp_size = lax.axis_size("inp")
    tm_size = lax.axis_size("tm")
    own_channels = CH // (inp_size * tm_size)
    widened = spectra.reshape(CH, 2, 1, inputs_here, spectra_here)
    received = lax.all_to_all(widened, ("inp", "tm"), split_axis=0, concat_axis=2, tiled=True)
    received = received.reshape(own_channels, 2, inp_size, tm_size, inputs_here, spectra_here)
    turned = received.transpose(0, 1, 2, 4, 3, 5).reshape(
        own_channels, 2, inp_size * inputs_here, tm_size * spectra_here
    )
    pol_size = lax.axis_size("pol")
    rows_here = turned.shape[2] // pol_size
    row_start = lax.axis_index("pol") * rows_here
    segment = lax.all_gather(turned, "pol", axis=3, tiled=True)
    own_rows = lax.dynamic_slice_in_dim(segment, row_start, rows_here, 2)
    left_rows = jnp.concatenate([own_rows[:, 0], own_rows[:, 1]], axis=-1)
    right_real = jnp.concatenate([segment[:, 0], segment[:, 1]], axis=-1)
    right_imag = jnp.concatenate([-segment[:, 1], segment[:, 0]], axis=-1)
    part_real = jnp.einsum(
        "crk,cjk->crj", left_rows, right_real, preferred_element_type=jnp.float32
    )
    part_imag = jnp.einsum(
        "crk,cjk->crj", left_rows, right_imag, preferred_element_type=jnp.float32
    )
    summed = jnp.stack([part_real, part_imag], axis=1)
    return summed * (1.0 / (turned.shape[3] * pol_size))


def solution(mesh):
    return jax.shard_map(
        per_device,
        mesh=mesh,
        in_specs=(P(("group", "inp"), ("tm", "pol")),),
        out_specs=P(("group", "inp", "tm"), None, "pol", None),
        check_vma=False,
    )
```

profile of v0, /device:TPU:0, one launch (start us, length us, event | category | flops | bytes accessed | tf_op | source)
XLA Modules:
  0.0 484.7 jit_solution(11061835007359937390)
XLA Ops:
  6.5 0.0 all-gather.2.cloned.1.call-start
  6.5 6.4 %copy.27 = bf16[128,16384]{0,1:T(8,128)(2,1)} copy(bf16[128,16384]{1,0:T(8,128)(2,1)} %param.1) | data formatting | bytes 8388608 | tf_op args[0]
  12.9 4.3 slice.163
  17.2 6.3 %copy.28 = bf16[128,15,1024]{2,0,1:T(8,128)(2,1)} copy(bf16[128,15,1024]{0,2,1:T(8,128)(2,1)} %slice.163) | data formatting | bytes 7864320 | tf_op jit(solution)/shard_map/slice | solution.py:41
  23.5 4.2 collective-permute-start
  27.8 1.1 multiply_reduce_fusion
  29.5 8.5 %negate_convert_fusion = (bf16[1024,512,1]{1,0,2:T(8,128)(2,1)S(1)}, bf16[1024,512,1]{1,0,2:T(8,128)(2,1)S(1)}) fusion(), kind=kLoop, calls=%fused_computation.62 | loop fusion | flops 8912896 | bytes 2097152 | tf_op jit(solution)/shard_map/convert.1
  38.1 0.2 pad_maximum_fusion.2
  38.3 4.1 copy.26
  42.4 2.7 convert_element_type.86
  45.1 0.5 broadcast_divide_fusion
  45.6 0.0 collective-permute-done
  45.6 6.2 %copy.29 = bf16[128,15,1024]{0,2,1:T(8,128)(2,1)} copy(bf16[128,15,1024]{2,0,1:T(8,128)(2,1)} %collective-permute-done) | data formatting | bytes 7864320 | tf_op jit(solution)/shard_map/ppermute | solution.py:14
  51.8 24.9 %add_convert_fusion = bf16[128,16,1024]{0,2,1:T(8,128)(2,1)} fusion(bf16[128,16,1024]{0,2,1:T(8,128)(2,1)} %bitcast.32, bf16[128,15,1024]{0,2,1:T(8,128)(2,1)} %copy.29, f32[1024]{0:T(1024)S(1)} %get-tuple-element.10, f32[1024]{0:T(1024)S(1)} %get-tuple-element.11, f32[1024]{0:T(1024)S(1)} %get-tuple-element.12, f32[1024]{0:T(1024)S(1)} %get-tuple-element.13, ...), kind=kLoop, calls=%fused_computation.37 | loop fusion | flops 132120576 | bytes 12386304 | tf_op jit(solution)/shard_map/convert_element_type | solution.py:50
  76.7 6.7 %copy.30 = bf16[128,16,1024]{2,1,0:T(8,128)(2,1)} copy(bf16[128,16,1024]{0,2,1:T(8,128)(2,1)} %add_convert_fusion) | data formatting | bytes 8388608 | tf_op jit(solution)/shard_map/convert_element_type | solution.py:50
  83.4 8.3 %convolution_convert_fusion = bf16[1024,2048]{1,0:T(8,128)(2,1)} fusion(bf16[1024,1024]{0,1:T(8,128)(2,1)S(1)} %convert_element_type.86, bf16[2048,1024]{1,0:T(8,128)(2,1)} %bitcast.34), kind=kOutput, calls=%fused_computation.54 | convolution fusion | flops 4297064448 | bytes 10485760 | tf_op jit(solution)/shard_map/dot_general | solution.py:51
  91.7 31.6 %reshape_reshape.3 = bf16[512,2,1,128,16]{4,3,1,0,2:T(8,128)(2,1)} reshape(bf16[1024,2048]{1,0:T(8,128)(2,1)} %convolution_convert_fusion) | data formatting | bytes 8388608 | tf_op jit(solution)/shard_map/reshape;reshape | solution.py:61
  123.2 24.9 %copy.31 = bf16[512,2,1,128,16]{3,4,2,1,0:T(8,128)(2,1)} copy(bf16[512,2,1,128,16]{4,3,1,0,2:T(8,128)(2,1)} %reshape_reshape.3) | data formatting | bytes 8388608 | tf_op jit(solution)/shard_map/reshape;reshape | solution.py:61
  148.1 124.0 %all_to_all.15 = bf16[512,2,1,128,16]{3,4,2,1,0:T(8,128)(2,1)S(1)} all-to-all(bf16[512,2,1,128,16]{3,4,2,1,0:T(8,128)(2,1)} %copy.31), channel_id=1, replica_groups=mesh['group'=2,'inp'=4,'tm'=2,'pol'=2] {'inp','tm'}, dimensions={0} | all-to-all | bytes 8388608 | tf_op jit(solution)/shard_map/all_to_all | solution.py:62
  272.1 5.3 %copy.40 = bf16[64,2,4,128,2,16]{3,2,0,1,5,4:T(4,128)(2,1)} copy(bf16[64,2,4,128,2,16]{3,5,1,0,4,2:T(8,128)(2,1)S(1)} %bitcast.33) | data formatting | bytes 8388608 | tf_op jit(solution)/shard_map/reshape | solution.py:64
  277.4 7.2 %reshape.135 = bf16[64,2,512,32]{2,0,1,3:T(8,128)(2,1)} reshape(bf16[64,2,4,128,2,16]{3,2,0,1,5,4:T(4,128)(2,1)} %copy.40) | data formatting | bytes 8388608 | tf_op jit(solution)/shard_map/reshape | solution.py:64
  284.6 0.0 all-gather.2.cloned.1.call-update
  284.6 19.0 %all-gather.2.cloned.1.call-done = bf16[64,2,512,64]{2,0,1,3:T(8,128)(2,1)} async-done(((bf16[64,2,512,32]{2,0,1,3:T(8,128)(2,1)}), bf16[64,2,512,64]{2,0,1,3:T(8,128)(2,1)}) %all-gather.2.cloned.1.call-update) | async-done | bytes 8388624 | tf_op jit(solution)/shard_map/all_gather | solution.py:70
  303.7 4.0 constant_dynamic-slice_fusion
  307.7 5.3 %copy.43 = bf16[64,1,256,64]{3,2,0,1:T(8,128)(2,1)} copy(bf16[64,1,256,64]{2,0,1,3:T(8,128)(2,1)} %get-tuple-element.5) | data formatting | bytes 4194304
  313.1 6.1 %fusion.29 = (bf16[64,1,512,64]{2,0,1,3:T(8,128)(2,1)}, bf16[64,1,512,64]{2,0,1,3:T(8,128)(2,1)}) fusion(bf16[64,2,512,64]{2,0,1,3:T(8,128)(2,1)} %all-gather.2.cloned.1.call-done), kind=kLoop, calls=%fused_computation.76 | loop fusion | bytes 16777216 | tf_op jit(solution)/shard_map/slice | solution.py:73
  319.2 9.2 %copy.46 = bf16[64,1,512,64]{3,2,0,1:T(8,128)(2,1)} copy(bf16[64,1,512,64]{2,0,1,3:T(8,128)(2,1)} %get-tuple-element.7) | data formatting | bytes 8388608
  328.4 3.8 copy.44
  332.2 7.7 %bitcast_negate_fusion = bf16[64,512,64]{2,1,0:T(8,128)(2,1)} fusion(bf16[64,1,512,64]{3,2,0,1:T(8,128)(2,1)} %copy.46), kind=kLoop, calls=%fused_computation.75 | loop fusion | flops 2097152 | bytes 8388608 | tf_op jit(solution)/shard_map/neg | solution.py:74
  339.9 9.3 %copy.45 = bf16[64,1,512,64]{3,2,0,1:T(8,128)(2,1)} copy(bf16[64,1,512,64]{2,0,1,3:T(8,128)(2,1)} %get-tuple-element.8) | data formatting | bytes 8388608
  349.2 0.0 copy-start
  349.2 22.8 %convolution_bitcast_fusion = f32[64,1,256,512]{3,2,0,1:T(8,128)} fusion(bf16[64,512,64]{2,1,0:T(8,128)(2,1)} %bitcast.24, bf16[64,512,64]{2,1,0:T(8,128)(2,1)} %bitcast_negate_fusion, bf16[64,256,64]{2,1,0:T(8,128)(2,1)} %bitcast.29, bf16[64,256,64]{2,1,0:T(8,128)(2,1)} %bitcast.27), kind=kOutput, calls=%fused_computation.29 | convolution fusion | flops 2172649472 | bytes 46137344 | tf_op jit(solution)/shard_map/crk,cjk->crj/dot_general | solution.py:78
  371.9 0.0 copy-done
  371.9 18.3 %convolution_bitcast_fusion.1 = f32[64,1,256,512]{3,2,0,1:T(8,128)} fusion(bf16[64,512,64]{2,1,0:T(8,128)(2,1)} %bitcast.26, bf16[64,512,64]{2,1,0:T(8,128)(2,1)S(1)} %bitcast.25, bf16[64,256,64]{2,1,0:T(8,128)(2,1)} %bitcast.30, bf16[64,256,64]{2,1,0:T(8,128)(2,1)} %bitcast.28), kind=kOutput, calls=%fused_computation.30 | convolution fusion | flops 2172649472 | bytes 46137344 | tf_op jit(solution)/shard_map/crk,cjk->crj/dot_general | solution.py:75
  390.3 43.6 %maximum_multiply_fusion = f32[64,2,256,512]{3,2,0,1:T(8,128)} fusion(f32[64,1,256,512]{3,2,0,1:T(8,128)} %convolution_bitcast_fusion, f32[64,1,256,512]{3,2,0,1:T(8,128)} %convolution_bitcast_fusion.1), kind=kLoop, calls=%fused_computation | loop fusion | flops 33554432 | bytes 134217728 | tf_op jit(solution)/shard_map/mul | solution.py:82
  433.9 44.0 %copy.38 = f32[64,2,256,512]{3,2,1,0:T(8,128)} copy(f32[64,2,256,512]{3,2,0,1:T(8,128)} %maximum_multiply_fusion) | data formatting | bytes 134217728 | tf_op jit(solution)/shard_map/mul | solution.py:82
  (1 shorter events, 0.0 us)
Async XLA Ops:
  6.5 297.2 %all-gather.2.cloned.1.call-start = ((), (), s32[]{:S(2)}) async-start(), calls=%async_computation.1 | async-start | bytes 12582912 | tf_op jit(solution)/shard_map/all_gather | solution.py:70
  23.5 22.1 %collective-permute-start = (bf16[128,15,1024]{2,0,1:T(8,128)(2,1)}, bf16[128,15,1024]{2,0,1:T(8,128)(2,1)}, u32[]{:S(2)}, u32[]{:S(2)}) collective-permute-start(bf16[128,15,1024]{2,0,1:T(8,128)(2,1)} %copy.28), channel_id=1, source_target_pairs={{0,1},{1,2},{2,3},{4,5},{5,6},{6,7},{8,9},{9,10},{10,11},{12,13},{... | collective-permute-start | bytes 11796488 | tf_op jit(solution)/shard_map/ppermute | solution.py:14
  349.2 22.8 %copy-start = (bf16[64,1,512,64]{3,2,0,1:T(8,128)(2,1)S(1)}, bf16[64,1,512,64]{3,2,0,1:T(8,128)(2,1)}, u32[]{:S(2)}) copy-start(bf16[64,1,512,64]{3,2,0,1:T(8,128)(2,1)} %copy.45) | copy-start | bytes 12582916
Sparse Core Ops, SparseCore 0:
  284.8 18.8 all-gather.1
where the time goes:
time: 488 us; the launch traced here: 485 us
  local copies, waits for them, and re-layouts  187 us (38%)
  blocking collectives  124 us (25%)
  other arithmetic  86.5 us (18%)
  matrix products  49.4 us (10%)
  waiting for transfers between devices  19.1 us (4%)
  between operations  14.1 us (3%)
    all_to_all x1, blocking collectives, per_device(): lax.all_to_all(widened, ('inp', 'tm'), split_axis=0, concat_axis=2, tiled...  124 us
    another operation x2, local copies, waits for them, and re-layouts, per_device(): widened = spectra.reshape(CH, 2, 1, inputs_here, spectra_here)  56.5 us
    mul x1, local copies, waits for them, and re-layouts, per_device(): return summed * (1.0 / (turned.shape[3] * pol_size))  44 us
    mul x1, other arithmetic, per_device(): return summed * (1.0 / (turned.shape[3] * pol_size))  43.6 us
    unnamed x7, local copies, waits for them, and re-layouts  34 us
    convert_element_type x1, other arithmetic, per_device(): filtered = filtered.astype(jnp.bfloat16)  24.9 us
    dot_general x1, matrix products, per_device(): jnp.einsum('crk,cjk->crj', left_rows, right_imag, preferred_element_type=...  22.8 us
    all_gather x1, waiting for transfers between devices, per_device(): segment = lax.all_gather(turned, 'pol', axis=3, tiled=True)  19 us
  transfers between devices with their start and end apart: 2, of which 1 were waited for; matrix products, arithmetic and copies ran while one was open for 4% of the time, Pallas kernels for 0%

commit v1 on v0

--- a/solution.py
+++ b/solution.py
@@ -67,7 +67,9 @@
     pol_size = lax.axis_size("pol")
     rows_here = turned.shape[2] // pol_size
     row_start = lax.axis_index("pol") * rows_here
-    segment = lax.all_gather(turned, "pol", axis=3, tiled=True)
+    segment = jnp.concatenate(
+        lax.all_to_all(jnp.stack([turned] * lax.axis_size("pol")), "pol", 0, 0), axis=3
+    )
     own_rows = lax.dynamic_slice_in_dim(segment, row_start, rows_here, 2)
     left_rows = jnp.concatenate([own_rows[:, 0], own_rows[:, 1]], axis=-1)
     right_real = jnp.concatenate([segment[:, 0], segment[:, 1]], axis=-1)

time: 488 us -> 492 us (level)
  blocking collectives: 124 us -> 18.5 us
  waiting for transfers between devices: 19.1 us -> 91.6 us
  starting transfers between devices: 4.24 us -> 36.7 us
  between operations: 14.1 us -> 0.73 us
  local copies, waits for them, and re-layouts: 187 us -> 198 us
  other arithmetic: 86.5 us -> 94.1 us
    all_to_all x1, blocking collectives: 124 us -> 18.5 us  [per_device(): lax.all_to_all(jnp.stack([turned] * lax.axis_size('pol')), 'pol', 0, 0)]
    all_to_all x0 -> x1, waiting for transfers between devices: none -> 91.6 us  [per_device(): lax.all_to_all(widened, ('inp', 'tm'), split_axis=0, concat_axis=2, tiled...]
    all_to_all x0 -> x1, starting transfers between devices: none -> 32.5 us  [per_device(): lax.all_to_all(widened, ('inp', 'tm'), split_axis=0, concat_axis=2, tiled...]
    all_gather x1 -> x0, waiting for transfers between devices: 19 us -> none  [per_device(): segment = lax.all_gather(turned, 'pol', axis=3, tiled=True)]
    transpose x0 -> x1, local copies, waits for them, and re-layouts: none -> 9.59 us  [per_device(): received.transpose(0, 1, 2, 4, 3, 5)]
    another operation x1 -> x2, other arithmetic: 8.54 us -> 16.2 us
    another operation x0 -> x1, local copies, waits for them, and re-layouts: none -> 7.18 us  [per_device(): jnp.stack([turned] * lax.axis_size('pol'))]
    reshape x2 -> x1, local copies, waits for them, and re-layouts: 12.5 us -> 8.44 us  [per_device(): jnp.concatenate(lax.all_to_all(jnp.stack([turned] * lax.axis_size('pol'))...]
where the time goes in v1:
time: 492 us; the launch traced here: 489 us
  local copies, waits for them, and re-layouts  198 us (40%)
  other arithmetic  94.1 us (19%)
  waiting for transfers between devices  91.6 us (19%)
  matrix products  49.2 us (10%)
  starting transfers between devices  36.7 us (7%)
  blocking collectives  18.5 us (4%)
    all_to_all x1, waiting for transfers between devices, per_device(): lax.all_to_all(widened, ('inp', 'tm'), split_axis=0, concat_axis=2, tiled...  91.6 us
    another operation x2, local copies, waits for them, and re-layouts, per_device(): widened = spectra.reshape(CH, 2, 1, inputs_here, spectra_here)  56.5 us
    mul x1, local copies, waits for them, and re-layouts, per_device(): return summed * (1.0 / (turned.shape[3] * pol_size))  44 us
    mul x1, other arithmetic, per_device(): return summed * (1.0 / (turned.shape[3] * pol_size))  43.6 us
    unnamed x9, local copies, waits for them, and re-layouts  33 us
    all_to_all x1, starting transfers between devices, per_device(): lax.all_to_all(widened, ('inp', 'tm'), split_axis=0, concat_axis=2, tiled...  32.5 us
    convert_element_type x1, other arithmetic, per_device(): filtered = filtered.astype(jnp.bfloat16)  24.9 us
    dot_general x1, matrix products, per_device(): jnp.einsum('crk,cjk->crj', left_rows, right_imag, preferred_element_type=...  22.8 us
  transfers between devices with their start and end apart: 2, of which 1 were waited for; matrix products, arithmetic and copies ran while one was open for 4% of the time, Pallas kernels for 0%

profile of v1, /device:TPU:0, one launch (start us, length us, event | category | flops | bytes accessed | tf_op | source)
XLA Modules:
  0.0 488.6 jit_solution(15606624826247650392)
XLA Ops:
  0.0 6.4 %copy.36 = bf16[128,16384]{0,1:T(8,128)(2,1)} copy(bf16[128,16384]{1,0:T(8,128)(2,1)} %param.1) | data formatting | bytes 8388608 | tf_op args[0]
  6.4 4.3 slice.163
  10.7 6.3 %copy.37 = bf16[128,15,1024]{2,0,1:T(8,128)(2,1)} copy(bf16[128,15,1024]{0,2,1:T(8,128)(2,1)} %slice.163) | data formatting | bytes 7864320 | tf_op jit(solution)/shard_map/slice | solution.py:41
  17.0 4.2 collective-permute-start
  21.2 1.1 multiply_reduce_fusion
  23.0 8.5 %negate_convert_fusion = (bf16[1024,512,1]{1,0,2:T(8,128)(2,1)S(1)}, bf16[1024,512,1]{1,0,2:T(8,128)(2,1)S(1)}) fusion(), kind=kLoop, calls=%fused_computation.63 | loop fusion | flops 8912896 | bytes 2097152 | tf_op jit(solution)/shard_map/convert.1
  31.6 0.2 pad_maximum_fusion.3
  31.8 4.1 copy.35
  35.8 2.7 convert_element_type.86
  38.6 0.5 broadcast_divide_fusion
  39.1 0.0 collective-permute-done
  39.1 6.2 %copy.38 = bf16[128,15,1024]{0,2,1:T(8,128)(2,1)} copy(bf16[128,15,1024]{2,0,1:T(8,128)(2,1)} %collective-permute-done) | data formatting | bytes 7864320 | tf_op jit(solution)/shard_map/ppermute | solution.py:14
  45.2 24.9 %add_convert_fusion = bf16[128,16,1024]{0,2,1:T(8,128)(2,1)} fusion(bf16[128,16,1024]{0,2,1:T(8,128)(2,1)} %bitcast.36, bf16[128,15,1024]{0,2,1:T(8,128)(2,1)} %copy.38, f32[1024]{0:T(1024)S(1)} %get-tuple-element.10, f32[1024]{0:T(1024)S(1)} %get-tuple-element.11, f32[1024]{0:T(1024)S(1)} %get-tuple-element.12, f32[1024]{0:T(1024)S(1)} %get-tuple-element.13, ...), kind=kLoop, calls=%fused_computation.38 | loop fusion | flops 132120576 | bytes 12386304 | tf_op jit(solution)/shard_map/convert_element_type | solution.py:50
  70.2 6.7 %copy.39 = bf16[128,16,1024]{2,1,0:T(8,128)(2,1)} copy(bf16[128,16,1024]{0,2,1:T(8,128)(2,1)} %add_convert_fusion) | data formatting | bytes 8388608 | tf_op jit(solution)/shard_map/convert_element_type | solution.py:50
  76.9 8.3 %convolution_convert_fusion = bf16[1024,2048]{1,0:T(8,128)(2,1)} fusion(bf16[1024,1024]{0,1:T(8,128)(2,1)S(1)} %convert_element_type.86, bf16[2048,1024]{1,0:T(8,128)(2,1)} %bitcast.38), kind=kOutput, calls=%fused_computation.55 | convolution fusion | flops 4297064448 | bytes 10485760 | tf_op jit(solution)/shard_map/dot_general | solution.py:51
  85.1 31.6 %reshape_reshape.3 = bf16[512,2,1,128,16]{4,3,1,0,2:T(8,128)(2,1)} reshape(bf16[1024,2048]{1,0:T(8,128)(2,1)} %convolution_convert_fusion) | data formatting | bytes 8388608 | tf_op jit(solution)/shard_map/reshape;reshape | solution.py:61
  116.7 24.9 %copy.40 = bf16[512,2,1,128,16]{3,4,2,1,0:T(8,128)(2,1)} copy(bf16[512,2,1,128,16]{4,3,1,0,2:T(8,128)(2,1)} %reshape_reshape.3) | data formatting | bytes 8388608 | tf_op jit(solution)/shard_map/reshape;reshape | solution.py:61
  141.6 32.5 %all-to-all-start = ((bf16[512,2,1,128,16]{3,4,2,1,0:T(8,128)(2,1)}), bf16[512,2,1,128,16]{3,4,2,1,0:T(8,128)(2,1)}, u32[]{:S(2)}, u32[]{:S(2)}) async-start(bf16[512,2,1,128,16]{3,4,2,1,0:T(8,128)(2,1)} %copy.40), calls=%async_computation | async-start | bytes 8388608 | tf_op jit(solution)/shard_map/all_to_all | solution.py:62
  174.1 91.6 %all-to-all-done = bf16[512,2,1,128,16]{3,4,2,1,0:T(8,128)(2,1)} async-done(((bf16[512,2,1,128,16]{3,4,2,1,0:T(8,128)(2,1)}), bf16[512,2,1,128,16]{3,4,2,1,0:T(8,128)(2,1)}, u32[]{:S(2)}, u32[]{:S(2)}) %all-to-all-start) | async-done | bytes 4194336 | tf_op jit(solution)/shard_map/all_to_all | solution.py:62
  265.7 9.6 %copy.42 = bf16[64,2,4,128,2,16]{3,2,5,4,1,0:T(4,128)(2,1)} copy(bf16[64,2,4,128,2,16]{3,5,1,0,4,2:T(8,128)(2,1)} %bitcast.6) | data formatting | bytes 8388608 | tf_op jit(solution)/shard_map/transpose | solution.py:64
  275.3 7.2 %stack_reshape.4 = bf16[1,64,2,512,32]{3,4,2,1,0:T(8,128)(2,1)} reshape(bf16[64,2,4,128,2,16]{3,2,5,4,1,0:T(4,128)(2,1)} %copy.42) | data formatting | bytes 8388608 | tf_op jit(solution)/shard_map/stack;reshape | solution.py:71
  282.5 7.6 %pad_maximum_fusion = bf16[2,64,2,512,32]{3,4,2,1,0:T(8,128)(2,1)} fusion(bf16[1,64,2,512,32]{3,4,2,1,0:T(8,128)(2,1)} %stack_reshape.4), kind=kLoop, calls=%fused_computation.31 | loop fusion | flops 4194304 | bytes 12582912 | tf_op jit(solution)/shard_map/stack | solution.py:71
  290.1 18.5 %all_to_all.20 = bf16[2,64,2,512,32]{3,4,2,1,0:T(8,128)(2,1)} all-to-all(bf16[2,64,2,512,32]{3,4,2,1,0:T(8,128)(2,1)} %pad_maximum_fusion), channel_id=1, replica_groups=mesh['group'=2,'inp'=4,'tm'=2,'pol'=2] {'pol'}, dimensions={0} | all-to-all | bytes 16777216 | tf_op jit(solution)/shard_map/all_to_all | solution.py:71
  308.6 8.4 %copy.43 = bf16[64,2,512,2,32]{2,4,3,1,0:T(8,128)(2,1)} copy(bf16[64,2,512,2,32]{2,4,1,0,3:T(8,128)(2,1)} %bitcast.37) | data formatting | bytes 16777216 | tf_op jit(solution)/shard_map/reshape | solution.py:70
  317.0 0.0 copy-start.1
  317.0 7.0 %fusion.29 = (bf16[64,1,512,64]{2,3,1,0:T(8,128)(2,1)}, bf16[64,1,512,64]{2,3,1,0:T(8,128)(2,1)}) fusion(bf16[64,2,512,64]{2,3,1,0:T(8,128)(2,1)} %bitcast.29), kind=kLoop, calls=%fused_computation.77 | loop fusion | bytes 16777216 | tf_op jit(solution)/shard_map/slice | solution.py:75
  324.1 1.8 copy-done.1
  325.8 1.7 constant_dynamic-slice_fusion
  327.5 4.9 copy.50
  332.4 8.4 %copy.53 = bf16[64,1,512,64]{3,2,0,1:T(8,128)(2,1)} copy(bf16[64,1,512,64]{2,3,1,0:T(8,128)(2,1)} %get-tuple-element.7) | data formatting | bytes 8388608
  340.8 3.2 copy.51
  344.0 7.7 %bitcast_negate_fusion = bf16[64,512,64]{2,1,0:T(8,128)(2,1)} fusion(bf16[64,1,512,64]{3,2,0,1:T(8,128)(2,1)} %copy.53), kind=kLoop, calls=%fused_computation.76 | loop fusion | flops 2097152 | bytes 8388608 | tf_op jit(solution)/shard_map/neg | solution.py:76
  351.7 8.4 %copy.52 = bf16[64,1,512,64]{3,2,0,1:T(8,128)(2,1)} copy(bf16[64,1,512,64]{2,3,1,0:T(8,128)(2,1)} %get-tuple-element.8) | data formatting | bytes 8388608
  360.1 0.0 copy-start
  360.1 22.8 %convolution_bitcast_fusion = f32[64,1,256,512]{3,2,0,1:T(8,128)} fusion(bf16[64,512,64]{2,1,0:T(8,128)(2,1)} %bitcast.26, bf16[64,512,64]{2,1,0:T(8,128)(2,1)} %bitcast_negate_fusion, bf16[64,256,64]{2,1,0:T(8,128)(2,1)} %bitcast.33, bf16[64,256,64]{2,1,0:T(8,128)(2,1)} %bitcast.31), kind=kOutput, calls=%fused_computation.29 | convolution fusion | flops 2172649472 | bytes 46137344 | tf_op jit(solution)/shard_map/crk,cjk->crj/dot_general | solution.py:80
  382.9 0.0 copy-done
  382.9 18.1 %convolution_bitcast_fusion.1 = f32[64,1,256,512]{3,2,0,1:T(8,128)} fusion(bf16[64,512,64]{2,1,0:T(8,128)(2,1)} %bitcast.28, bf16[64,512,64]{2,1,0:T(8,128)(2,1)S(1)} %bitcast.27, bf16[64,256,64]{2,1,0:T(8,128)(2,1)} %bitcast.34, bf16[64,256,64]{2,1,0:T(8,128)(2,1)} %bitcast.32), kind=kOutput, calls=%fused_computation.30 | convolution fusion | flops 2172649472 | bytes 46137344 | tf_op jit(solution)/shard_map/crk,cjk->crj/dot_general | solution.py:77
  401.0 43.6 %maximum_multiply_fusion = f32[64,2,256,512]{3,2,0,1:T(8,128)} fusion(f32[64,1,256,512]{3,2,0,1:T(8,128)} %convolution_bitcast_fusion, f32[64,1,256,512]{3,2,0,1:T(8,128)} %convolution_bitcast_fusion.1), kind=kLoop, calls=%fused_computation | loop fusion | flops 33554432 | bytes 134217728 | tf_op jit(solution)/shard_map/mul | solution.py:84
  444.6 44.0 %copy.47 = f32[64,2,256,512]{3,2,1,0:T(8,128)} copy(f32[64,2,256,512]{3,2,0,1:T(8,128)} %maximum_multiply_fusion) | data formatting | bytes 134217728 | tf_op jit(solution)/shard_map/mul | solution.py:84
  (1 shorter events, 0.0 us)
Async XLA Ops:
  17.0 22.1 %collective-permute-start = (bf16[128,15,1024]{2,0,1:T(8,128)(2,1)}, bf16[128,15,1024]{2,0,1:T(8,128)(2,1)}, u32[]{:S(2)}, u32[]{:S(2)}) collective-permute-start(bf16[128,15,1024]{2,0,1:T(8,128)(2,1)} %copy.37), channel_id=1, source_target_pairs={{0,1},{1,2},{2,3},{4,5},{5,6},{6,7},{8,9},{9,10},{10,11},{12,13},{... | collective-permute-start | bytes 11796488 | tf_op jit(solution)/shard_map/ppermute | solution.py:14
  141.6 124.1 %all-to-all-start = ((bf16[512,2,1,128,16]{3,4,2,1,0:T(8,128)(2,1)}), bf16[512,2,1,128,16]{3,4,2,1,0:T(8,128)(2,1)}, u32[]{:S(2)}, u32[]{:S(2)}) async-start(bf16[512,2,1,128,16]{3,4,2,1,0:T(8,128)(2,1)} %copy.40), calls=%async_computation | async-start | bytes 8388608 | tf_op jit(solution)/shard_map/all_to_all | solution.py:62
  317.0 8.8 %copy-start.1 = (bf16[64,2,512,2,32]{2,4,3,1,0:T(8,128)(2,1)S(1)}, bf16[64,2,512,2,32]{2,4,3,1,0:T(8,128)(2,1)}, u32[]{:S(2)}) copy-start(bf16[64,2,512,2,32]{2,4,3,1,0:T(8,128)(2,1)} %copy.43) | copy-start | bytes 25165828
  360.1 22.8 %copy-start = (bf16[64,1,512,64]{3,2,0,1:T(8,128)(2,1)S(1)}, bf16[64,1,512,64]{3,2,0,1:T(8,128)(2,1)}, u32[]{:S(2)}) copy-start(bf16[64,1,512,64]{3,2,0,1:T(8,128)(2,1)} %copy.52) | copy-start | bytes 12582916
